TPU v7x, 32 devices: a whole 2x2x4 slice. The times are simulated.
32 devices in a mesh: sub: 8 (over z, x), grp: 4 (over y, core).
Axes of the slice: x: 2, y: 2, z: 4, core: 2. Of those that a mesh axis runs over, the one named last changes fastest.
Arguments:
- resid: float32 [32768, 256], P(('sub', 'grp')), may hold values from -6 to 6
- schur_inv: bfloat16 [65536, 2048], P(('sub', 'grp')), may hold values from -0.125 to 0.125
- basis: bfloat16 [512, 2048], P(('sub', 'grp')), may hold values from -1.5 to 1.5
- scaling: float32 [65536], P(('sub', 'grp')), may hold values from 0.25 to 1
- coarse_inv: bfloat16 [512, 512], P(('sub', 'grp')), may hold values from -0.5 to 0.5
- source_row: int32 [65536], P(('sub', 'grp')), may hold values from 0 to 3071, as said below
- primal_idx: int32 [512], P(('sub', 'grp')), may hold values from 0 to 2047, as said below
Outputs:
- first_apply: float32 [32768, 256], P(('sub', 'grp'))
- second_apply: float32 [32768, 256], P(('sub', 'grp'))
Inputs may be any that keep to these rules, and one draw needn't show every extreme that they name: `source_row`: within one subdomain the entries are distinct; the first subdomain of each chain has none below 1024, the last none at or above 2048. `primal_idx`: within one subdomain the entries are distinct.
All inputs are finite; a program needn't handle non-finite values.
Results may differ from a plain program's by a relative error of at most 0.0076.
Values may be sent and summed in bfloat16 or wider, within the bound.
No kernel may reach another device: no remote copies, remote signals or barrier semaphores. Data moves between devices by JAX's collectives and lax.ppermute only.
A program may use at most 64 MiB of HBM per device.

v0:
```python
import jax
import jax.numpy as jnp
from jax import lax
from jax.sharding import PartitionSpec as P


def with_halo(cells, sides, width):
    for axis, dim in sides:
        count = lax.axis_size(axis)
        ends = count - 1
        head = lax.slice_in_dim(cells, 0, width, axis=dim)
        tail = lax.slice_in_dim(cells, cells.shape[dim] - width, cells.shape[dim], axis=dim)
        cells = jnp.concatenate(
            [
                lax.ppermute(tail, axis, [(i, (i + 1) % count) for i in range(ends)]),
                cells,
                lax.ppermute(head, axis, [((i + 1) % count, i) for i in range(ends)]),
            ],
            axis=dim,
        )
    return cells


def shifted(shard, axis, by):
    devices = lax.axis_size(axis)
    pairs = [(i, i + by) for i in range(devices) if 0 <= i + by < devices]
    return lax.ppermute(shard, axis, pairs)


def shards(resid, schur_inv, basis, scaling, coarse_inv, source_row, primal_idx):
    own_count = resid.shape[0]
    scale_column = scaling[:, None]

    def add_all(portion):
        return jnp.dot(coarse_inv, portion, preferred_element_type=jnp.float32)

    def precondition(vector_in):
        rounded = vector_in.astype(jnp.bfloat16)
        padded = with_halo(rounded, (("sub", 0),), own_count)
        gathered = padded[source_row]
        scaled = (scale_column * gathered.astype(jnp.float32)).astype(jnp.bfloat16)
        primal = scaled[primal_idx]
        idx = lax.axis_index("sub") * lax.axis_size("grp") + lax.axis_index("grp")
        total = lax.axis_size("sub") * lax.axis_size("grp") * primal.shape[0]
        buf = lax.dynamic_update_slice(
            jnp.zeros((total, primal.shape[1]), primal.dtype), primal, (idx * primal.shape[0], 0)
        )
        coarse = add_all(lax.psum(buf, ("sub", "grp")))
        coarse_rounded = coarse.astype(jnp.bfloat16)
        solved = jnp.dot(schur_inv, scaled, preferred_element_type=jnp.float32)
        solved = solved + lax.dot_general(
            basis, coarse_rounded, (((0,), (0,)), ((), ())), preferred_element_type=jnp.float32
        )
        weighted = (scale_column * solved).astype(jnp.bfloat16)
        spread = (
            jnp.zeros((3 * own_count, weighted.shape[1]), jnp.bfloat16).at[source_row].set(weighted)
        )
        from_next = shifted(spread[:own_count], "sub", -1)
        from_previous = shifted(spread[2 * own_count :], "sub", 1)
        return (
            spread[own_count : 2 * own_count].astype(jnp.float32)
            + from_next.astype(jnp.float32)
            + from_previous.astype(jnp.float32)
        )

    first_apply = precondition(resid)
    second_apply = precondition(first_apply)
    return (first_apply, second_apply)


def solution(mesh):
    return jax.shard_map(
        shards,
        mesh=mesh,
        in_specs=(
            P(("sub", "grp"), None),
            P(("sub", "grp"), None),
            P(("sub", "grp"), None),
            P(("sub", "grp")),
            P(("sub", "grp"), None),
            P(("sub", "grp")),
            P(("sub", "grp")),
        ),
        out_specs=(P(("sub", "grp"), None), P(("sub", "grp"), None)),
        check_vma=False,
    )
```

profile of v0, /device:TPU:0, one launch (start us, length us, event | category | flops | bytes accessed | tf_op | source)
XLA Modules:
  0.0 418.4 jit_solution(4887360545982959692)
XLA Ops:
  7.2 0.0 copy-start
  7.2 0.0 all-reduce.3.cloned.1.call-start
  7.2 1.3 convert_element_type.56
  8.5 1.3 collective-permute-start.1
  9.8 5.5 %collective-permute-start = (bf16[1024,256]{1,0:T(8,128)(2,1)S(1)}, bf16[1024,256]{1,0:T(8,128)(2,1)S(1)}, u32[]{:S(2)}, u32[]{:S(2)}) collective-permute-start(bf16[1024,256]{1,0:T(8,128)(2,1)S(1)} %convert_element_type.56), channel_id=1, source_target_pairs={{0,4},{4,8},{8,12},{12,16},{16,20},{20,24},{24,28},{1,5},{5,9},{9,... | collective-permute-start | bytes 1572872 | tf_op jit(solution)/shard_map/ppermute | solution.py:15
  15.3 0.7 compare_select_fusion.1
  16.0 0.7 broadcast_clamp_fusion
  16.7 8.6 %collective-permute-done.1 = bf16[1024,256]{1,0:T(8,128)(2,1)S(1)} collective-permute-done((bf16[1024,256]{1,0:T(8,128)(2,1)S(1)}, bf16[1024,256]{1,0:T(8,128)(2,1)S(1)}, u32[]{:S(2)}, u32[]{:S(2)}) %collective-permute-start.1) | collective-permute-done | bytes 524320 | tf_op jit(solution)/shard_map/ppermute | solution.py:17
  25.3 11.4 %collective-permute-done = bf16[1024,256]{1,0:T(8,128)(2,1)S(1)} collective-permute-done((bf16[1024,256]{1,0:T(8,128)(2,1)S(1)}, bf16[1024,256]{1,0:T(8,128)(2,1)S(1)}, u32[]{:S(2)}, u32[]{:S(2)}) %collective-permute-start) | collective-permute-done | bytes 524320 | tf_op jit(solution)/shard_map/ppermute | solution.py:15
  36.7 0.1 pad_maximum_fusion
  36.8 0.0 copy-start.3
  36.8 7.5 %gather_fusion = bf16[2048,256]{1,0:T(8,128)(2,1)S(1)} fusion(bf16[3072,256]{1,0:T(8,128)(2,1)S(1)} %pad_maximum_fusion, s32[2048]{0:T(1024)S(1)} %get-tuple-element.8), kind=kCustom, calls=%fused_computation | custom fusion | bytes 2105344 | tf_op jit(solution)/shard_map/gather | solution.py:40
  44.3 0.0 copy-done.3
  44.3 0.3 multiply_convert_fusion.1
  44.6 0.6 gather_fusion.1
  45.3 0.0 copy-start.2
  45.3 0.7 copy-done.2
  46.0 0.0 all-reduce.3.cloned.1.call-update
  46.0 0.0 copy-start.4
  46.0 0.0 all-reduce.5.cloned.1.call-start
  46.1 5.8 %fusion.13 = f32[256,2048]{1,0:T(8,128)S(1)} fusion(bf16[2048,256]{1,0:T(8,128)(2,1)S(1)} %multiply_convert_fusion.1, bf16[2048,2048]{1,0:T(8,128)(2,1)} %param.8), kind=kOutput, calls=%fused_computation.35 | convolution fusion | flops 2147483648 | bytes 11534336 | tf_op jit(solution)/shard_map/dot_general | solution.py:50
  51.8 120.6 %all-reduce.3.cloned.1.call-done = bf16[512,256]{1,0:T(8,128)(2,1)} async-done(((bf16[512,256]{1,0:T(8,128)(2,1)}), bf16[512,256]{1,0:T(8,128)(2,1)}) %all-reduce.3.cloned.1.call-update) | async-done | bytes 262160 | tf_op jit(solution)/shard_map/psum | solution.py:48
  172.4 0.0 copy-done
  172.4 0.0 copy-done.4
  172.4 1.7 fusion.5
  174.1 0.5 copy.9
  174.6 9.8 %scatter_custom_fusion = bf16[3072,256]{1,0:T(8,128)(2,1)S(1)} fusion(s32[2048]{0:T(1024)S(1)} %get-tuple-element.9, bf16[2048,256]{1,0:T(8,128)(2,1)S(1)} %copy.9, bf16[]{:T(256)} %constant.10.clone.1), kind=kCustom, calls=%fused_computation.24 | custom fusion | bytes 1572866 | tf_op jit(solution)/shard_map/scatter | solution.py:56
  184.4 0.1 fusion.12
  184.5 1.3 collective-permute-start.2
  185.8 4.6 %collective-permute-start.3 = (bf16[1024,256]{1,0:T(8,128)(2,1)S(1)}, bf16[1024,256]{1,0:T(8,128)(2,1)S(1)}, u32[]{:S(2)}, u32[]{:S(2)}) collective-permute-start(bf16[1024,256]{1,0:T(8,128)(2,1)S(1)} %get-tuple-element.7), channel_id=1, source_target_pairs={{0,4},{4,8},{8,12},{12,16},{16,20},{20,24},{24,28},{1,5},{5,9},{9,... | collective-permute-start | bytes 1572872 | tf_op jit(solution)/shard_map/ppermute | solution.py:27
  190.4 8.9 %collective-permute-done.2 = bf16[1024,256]{1,0:T(8,128)(2,1)S(1)} collective-permute-done((bf16[1024,256]{1,0:T(8,128)(2,1)S(1)}, bf16[1024,256]{1,0:T(8,128)(2,1)S(1)}, u32[]{:S(2)}, u32[]{:S(2)}) %collective-permute-start.2) | collective-permute-done | bytes 524320 | tf_op jit(solution)/shard_map/ppermute | solution.py:27
  199.3 11.1 %collective-permute-done.3 = bf16[1024,256]{1,0:T(8,128)(2,1)S(1)} collective-permute-done((bf16[1024,256]{1,0:T(8,128)(2,1)S(1)}, bf16[1024,256]{1,0:T(8,128)(2,1)S(1)}, u32[]{:S(2)}, u32[]{:S(2)}) %collective-permute-start.3) | collective-permute-done | bytes 524320 | tf_op jit(solution)/shard_map/ppermute | solution.py:27
  210.4 1.2 fusion.10
  211.5 1.3 collective-permute-start.5
  212.8 5.2 %collective-permute-start.4 = (bf16[1024,256]{1,0:T(8,128)(2,1)S(1)}, bf16[1024,256]{1,0:T(8,128)(2,1)S(1)}, u32[]{:S(2)}, u32[]{:S(2)}) collective-permute-start(bf16[1024,256]{1,0:T(8,128)(2,1)S(1)} %get-tuple-element.2), channel_id=1, source_target_pairs={{0,4},{4,8},{8,12},{12,16},{16,20},{20,24},{24,28},{1,5},{5,9},{9,... | collective-permute-start | bytes 1572872 | tf_op jit(solution)/shard_map/ppermute | solution.py:15
  218.0 10.0 %collective-permute-done.5 = bf16[1024,256]{1,0:T(8,128)(2,1)S(1)} collective-permute-done((bf16[1024,256]{1,0:T(8,128)(2,1)S(1)}, bf16[1024,256]{1,0:T(8,128)(2,1)S(1)}, u32[]{:S(2)}, u32[]{:S(2)}) %collective-permute-start.5) | collective-permute-done | bytes 524320 | tf_op jit(solution)/shard_map/ppermute | solution.py:17
  228.0 11.4 %collective-permute-done.4 = bf16[1024,256]{1,0:T(8,128)(2,1)S(1)} collective-permute-done((bf16[1024,256]{1,0:T(8,128)(2,1)S(1)}, bf16[1024,256]{1,0:T(8,128)(2,1)S(1)}, u32[]{:S(2)}, u32[]{:S(2)}) %collective-permute-start.4) | collective-permute-done | bytes 524320 | tf_op jit(solution)/shard_map/ppermute | solution.py:15
  239.4 0.1 pad_maximum_fusion.1
  239.5 7.5 %gather_fusion.2 = bf16[2048,256]{1,0:T(8,128)(2,1)S(1)} fusion(bf16[3072,256]{1,0:T(8,128)(2,1)S(1)} %pad_maximum_fusion.1, s32[2048]{0:T(1024)S(1)} %get-tuple-element.8), kind=kCustom, calls=%fused_computation.2 | custom fusion | bytes 2105344 | tf_op jit(solution)/shard_map/gather | solution.py:40
  247.0 0.3 multiply_convert_fusion
  247.3 0.6 gather_fusion.3
  248.0 0.0 copy-start.1
  248.0 0.7 copy-done.1
  248.7 0.0 all-reduce.5.cloned.1.call-update
  248.7 5.8 %fusion.14 = f32[256,2048]{1,0:T(8,128)S(1)} fusion(bf16[2048,256]{1,0:T(8,128)(2,1)S(1)} %multiply_convert_fusion, bf16[2048,2048]{1,0:T(8,128)(2,1)} %param.8), kind=kOutput, calls=%fused_computation.36 | convolution fusion | flops 2147483648 | bytes 11534336 | tf_op jit(solution)/shard_map/dot_general | solution.py:50
  254.5 118.0 %all-reduce.5.cloned.1.call-done = bf16[512,256]{1,0:T(8,128)(2,1)} async-done(((bf16[512,256]{1,0:T(8,128)(2,1)}), bf16[512,256]{1,0:T(8,128)(2,1)}) %all-reduce.5.cloned.1.call-update) | async-done | bytes 262160 | tf_op jit(solution)/shard_map/psum | solution.py:48
  372.5 1.7 fusion.4
  374.1 0.5 copy.10
  374.7 9.8 %scatter_custom_fusion.1 = bf16[3072,256]{1,0:T(8,128)(2,1)S(1)} fusion(s32[2048]{0:T(1024)S(1)} %get-tuple-element.9, bf16[2048,256]{1,0:T(8,128)(2,1)S(1)} %copy.10, bf16[]{:T(256)} %constant.10.clone.1), kind=kCustom, calls=%fused_computation.22 | custom fusion | bytes 1572866 | tf_op jit(solution)/shard_map/scatter | solution.py:56
  384.5 0.1 fusion.11
  384.5 1.3 collective-permute-start.6
  385.8 4.6 %collective-permute-start.7 = (bf16[1024,256]{1,0:T(8,128)(2,1)S(1)}, bf16[1024,256]{1,0:T(8,128)(2,1)S(1)}, u32[]{:S(2)}, u32[]{:S(2)}) collective-permute-start(bf16[1024,256]{1,0:T(8,128)(2,1)S(1)} %get-tuple-element.5), channel_id=1, source_target_pairs={{0,4},{4,8},{8,12},{12,16},{16,20},{20,24},{24,28},{1,5},{5,9},{9,... | collective-permute-start | bytes 1572872 | tf_op jit(solution)/shard_map/ppermute | solution.py:27
  390.4 8.9 %collective-permute-done.6 = bf16[1024,256]{1,0:T(8,128)(2,1)S(1)} collective-permute-done((bf16[1024,256]{1,0:T(8,128)(2,1)S(1)}, bf16[1024,256]{1,0:T(8,128)(2,1)S(1)}, u32[]{:S(2)}, u32[]{:S(2)}) %collective-permute-start.6) | collective-permute-done | bytes 524320 | tf_op jit(solution)/shard_map/ppermute | solution.py:27
  399.3 11.1 %collective-permute-done.7 = bf16[1024,256]{1,0:T(8,128)(2,1)S(1)} collective-permute-done((bf16[1024,256]{1,0:T(8,128)(2,1)S(1)}, bf16[1024,256]{1,0:T(8,128)(2,1)S(1)}, u32[]{:S(2)}, u32[]{:S(2)}) %collective-permute-start.7) | collective-permute-done | bytes 524320 | tf_op jit(solution)/shard_map/ppermute | solution.py:27
  410.4 1.1 convert_add_fusion
  (5 shorter events, 0.1 us)
Async XLA Ops:
  7.2 165.2 %copy-start = (bf16[16,2048]{1,0:T(8,128)(2,1)S(1)}, bf16[16,2048]{1,0:T(8,128)(2,1)}, u32[]{:S(2)}) copy-start(bf16[16,2048]{1,0:T(8,128)(2,1)} %param.9) | copy-start | bytes 196612
  7.2 165.2 %all-reduce.3.cloned.1.call-start = ((), (), s32[]{:S(2)}) async-start(), calls=%async_computation | async-start | bytes 524288 | tf_op jit(solution)/shard_map/psum | solution.py:48
  8.5 16.8 %collective-permute-start.1 = (bf16[1024,256]{1,0:T(8,128)(2,1)S(1)}, bf16[1024,256]{1,0:T(8,128)(2,1)S(1)}, u32[]{:S(2)}, u32[]{:S(2)}) collective-permute-start(bf16[1024,256]{1,0:T(8,128)(2,1)S(1)} %convert_element_type.56), channel_id=1, source_target_pairs={{4,0},{8,4},{12,8},{16,12},{20,16},{24,20},{28,24},{5,1},{9,5},{13... | collective-permute-start | bytes 1572872 | tf_op jit(solution)/shard_map/ppermute | solution.py:17
  9.8 26.8 %collective-permute-start = (bf16[1024,256]{1,0:T(8,128)(2,1)S(1)}, bf16[1024,256]{1,0:T(8,128)(2,1)S(1)}, u32[]{:S(2)}, u32[]{:S(2)}) collective-permute-start(bf16[1024,256]{1,0:T(8,128)(2,1)S(1)} %convert_element_type.56), channel_id=1, source_target_pairs={{0,4},{4,8},{8,12},{12,16},{16,20},{20,24},{24,28},{1,5},{5,9},{9,... | collective-permute-start | bytes 1572872 | tf_op jit(solution)/shard_map/ppermute | solution.py:15
  36.8 7.5 %copy-start.3 = (f32[2048]{0:T(1024)S(1)}, f32[2048]{0:T(1024)}, u32[]{:S(2)}) copy-start(f32[2048]{0:T(1024)} %param.10) | copy-start | bytes 24580
  45.3 0.7 copy-start.2
  46.0 126.4 %copy-start.4 = (bf16[16,512]{1,0:T(8,128)(2,1)S(1)}, bf16[16,512]{1,0:T(8,128)(2,1)}, u32[]{:S(2)}) copy-start(bf16[16,512]{1,0:T(8,128)(2,1)} %param.11) | copy-start | bytes 49156
  46.0 326.5 %all-reduce.5.cloned.1.call-start = ((), (), s32[]{:S(2)}) async-start(), calls=%async_computation.1 | async-start | bytes 524288 | tf_op jit(solution)/shard_map/psum | solution.py:48
  184.5 14.8 %collective-permute-start.2 = (bf16[1024,256]{1,0:T(8,128)(2,1)S(1)}, bf16[1024,256]{1,0:T(8,128)(2,1)S(1)}, u32[]{:S(2)}, u32[]{:S(2)}) collective-permute-start(bf16[1024,256]{1,0:T(8,128)(2,1)S(1)} %get-tuple-element.6), channel_id=1, source_target_pairs={{4,0},{8,4},{12,8},{16,12},{20,16},{24,20},{28,24},{5,1},{9,5},{13... | collective-permute-start | bytes 1572872 | tf_op jit(solution)/shard_map/ppermute | solution.py:27
  185.8 24.6 %collective-permute-start.3 = (bf16[1024,256]{1,0:T(8,128)(2,1)S(1)}, bf16[1024,256]{1,0:T(8,128)(2,1)S(1)}, u32[]{:S(2)}, u32[]{:S(2)}) collective-permute-start(bf16[1024,256]{1,0:T(8,128)(2,1)S(1)} %get-tuple-element.7), channel_id=1, source_target_pairs={{0,4},{4,8},{8,12},{12,16},{16,20},{20,24},{24,28},{1,5},{5,9},{9,... | collective-permute-start | bytes 1572872 | tf_op jit(solution)/shard_map/ppermute | solution.py:27
  211.5 16.5 %collective-permute-start.5 = (bf16[1024,256]{1,0:T(8,128)(2,1)S(1)}, bf16[1024,256]{1,0:T(8,128)(2,1)S(1)}, u32[]{:S(2)}, u32[]{:S(2)}) collective-permute-start(bf16[1024,256]{1,0:T(8,128)(2,1)S(1)} %get-tuple-element.2), channel_id=1, source_target_pairs={{4,0},{8,4},{12,8},{16,12},{20,16},{24,20},{28,24},{5,1},{9,5},{13... | collective-permute-start | bytes 1572872 | tf_op jit(solution)/shard_map/ppermute | solution.py:17
  212.8 26.6 %collective-permute-start.4 = (bf16[1024,256]{1,0:T(8,128)(2,1)S(1)}, bf16[1024,256]{1,0:T(8,128)(2,1)S(1)}, u32[]{:S(2)}, u32[]{:S(2)}) collective-permute-start(bf16[1024,256]{1,0:T(8,128)(2,1)S(1)} %get-tuple-element.2), channel_id=1, source_target_pairs={{0,4},{4,8},{8,12},{12,16},{16,20},{20,24},{24,28},{1,5},{5,9},{9,... | collective-permute-start | bytes 1572872 | tf_op jit(solution)/shard_map/ppermute | solution.py:15
  248.0 0.7 copy-start.1
  384.5 14.8 %collective-permute-start.6 = (bf16[1024,256]{1,0:T(8,128)(2,1)S(1)}, bf16[1024,256]{1,0:T(8,128)(2,1)S(1)}, u32[]{:S(2)}, u32[]{:S(2)}) collective-permute-start(bf16[1024,256]{1,0:T(8,128)(2,1)S(1)} %get-tuple-element.4), channel_id=1, source_target_pairs={{4,0},{8,4},{12,8},{16,12},{20,16},{24,20},{28,24},{5,1},{9,5},{13... | collective-permute-start | bytes 1572872 | tf_op jit(solution)/shard_map/ppermute | solution.py:27
  385.8 24.6 %collective-permute-start.7 = (bf16[1024,256]{1,0:T(8,128)(2,1)S(1)}, bf16[1024,256]{1,0:T(8,128)(2,1)S(1)}, u32[]{:S(2)}, u32[]{:S(2)}) collective-permute-start(bf16[1024,256]{1,0:T(8,128)(2,1)S(1)} %get-tuple-element.5), channel_id=1, source_target_pairs={{0,4},{4,8},{8,12},{12,16},{16,20},{20,24},{24,28},{1,5},{5,9},{9,... | collective-permute-start | bytes 1572872 | tf_op jit(solution)/shard_map/ppermute | solution.py:27
Sparse Core Ops, SparseCore 0:
  46.1 126.2 all-reduce.2
  248.8 123.6 all-reduce.4
where the time goes:
time: 419 us; the launch traced here: 418 us
  waiting for transfers between devices  320 us (76%)
  local copies, waits for them, and re-layouts  38.4 us (9%)
  starting transfers between devices  25.1 us (6%)
  matrix products  14.9 us (4%)
  between operations  14.3 us (3%)
  other arithmetic  5.82 us (1%)
    psum x2, waiting for transfers between devices, precondition(): coarse = add_all(lax.psum(buf, ('sub', 'grp')))  239 us
    ppermute x4, waiting for transfers between devices, shifted(): return lax.ppermute(shard, axis, pairs)  40 us
    ppermute x2, waiting for transfers between devices, with_halo(): lax.ppermute(tail, axis, [(i, (i + 1) % count) for i in range(ends)])  22.8 us
    scatter x2, local copies, waits for them, and re-layouts, precondition(): jnp.zeros((3 * own_count, weighted.shape[1]), jnp.bfloat16).at[source_row]  19.6 us
    ppermute x2, waiting for transfers between devices, with_halo(): lax.ppermute(head, axis, [((i + 1) % count, i) for i in range(ends)])  18.5 us
    gather x2, local copies, waits for them, and re-layouts, precondition(): gathered = padded[source_row]  15 us
    ppermute x4, starting transfers between devices, shifted(): return lax.ppermute(shard, axis, pairs)  11.7 us
    dot_general x2, matrix products, precondition(): solved = jnp.dot(schur_inv, scaled, preferred_element_type=jnp.float32)  11.5 us
  transfers between devices with their start and end apart: 10, of which 10 were waited for; matrix products, arithmetic and copies ran while one was open for 3% of the time, Pallas kernels for 0%

commit v1 on v0

--- a/solution.py
+++ b/solution.py
@@ -2,6 +2,12 @@
 import jax.numpy as jnp
 from jax import lax
 from jax.sharding import PartitionSpec as P
+
+
+def summed_here(shard, mesh_axis):
+    blocks = lax.all_gather(shard, mesh_axis, axis=0, tiled=False)
+    total = blocks.sum(axis=0)
+    return total
 
 
 def with_halo(cells, sides, width):
@@ -45,7 +51,7 @@
         buf = lax.dynamic_update_slice(
             jnp.zeros((total, primal.shape[1]), primal.dtype), primal, (idx * primal.shape[0], 0)
         )
-        coarse = add_all(lax.psum(buf, ("sub", "grp")))
+        coarse = add_all(summed_here(buf, ("sub", "grp")))
         coarse_rounded = coarse.astype(jnp.bfloat16)
         solved = jnp.dot(schur_inv, scaled, preferred_element_type=jnp.float32)
         solved = solved + lax.dot_general(

time: 419 us -> 335 us (0.80)
  waiting for transfers between devices: 320 us -> 228 us
  other arithmetic: 5.82 us -> 15.3 us
    psum x2 -> x0, waiting for transfers between devices: 239 us -> none  [precondition(): coarse = add_all(lax.psum(buf, ('sub', 'grp')))]
    all_gather x0 -> x2, waiting for transfers between devices: none -> 145 us  [summed_here(): blocks = lax.all_gather(shard, mesh_axis, axis=0, tiled=False)]
    reduce_sum x0 -> x2, other arithmetic: none -> 9.5 us  [summed_here(): total = blocks.sum(axis=0)]
  transfers between devices with their start and end apart: 10 -> 10, of which waited for: 10 -> 10; matrix products, arithmetic and copies ran while one was open for 3% -> 4% of each run, Pallas kernels for 0% -> 0%
where the time goes in v1:
time: 335 us
  waiting for transfers between devices  228 us (68%)
  local copies, waits for them, and re-layouts  38.4 us (11%)
  starting transfers between devices  25.1 us (7%)
  other arithmetic  15.3 us (5%)
  between operations  14.3 us (4%)
  matrix products  13 us (4%)
    all_gather x2, waiting for transfers between devices, summed_here(): blocks = lax.all_gather(shard, mesh_axis, axis=0, tiled=False)  145 us
    ppermute x4, waiting for transfers between devices, shifted(): return lax.ppermute(shard, axis, pairs)  42.4 us
    ppermute x2, waiting for transfers between devices, with_halo(): lax.ppermute(tail, axis, [(i, (i + 1) % count) for i in range(ends)])  22.8 us
    scatter x2, local copies, waits for them, and re-layouts, precondition(): jnp.zeros((3 * own_count, weighted.shape[1]), jnp.bfloat16).at[source_row]  19.6 us
    ppermute x2, waiting for transfers between devices, with_halo(): lax.ppermute(head, axis, [((i + 1) % count, i) for i in range(ends)])  18.5 us
    gather x2, local copies, waits for them, and re-layouts, precondition(): gathered = padded[source_row]  15 us
    ppermute x4, starting transfers between devices, shifted(): return lax.ppermute(shard, axis, pairs)  11.7 us
    dot_general x2, matrix products, precondition(): solved = jnp.dot(schur_inv, scaled, preferred_element_type=jnp.float32)  11.5 us
  transfers between devices with their start and end apart: 10, of which 10 were waited for; matrix products, arithmetic and copies ran while one was open for 4% of the time, Pallas kernels for 0%

profile of v1, /device:TPU:0, one launch (start us, length us, event | category | flops | bytes accessed | tf_op | source)
XLA Modules:
  0.0 334.5 jit_solution(5866729613659919513)
XLA Ops:
  7.2 0.0 copy-start
  7.2 0.0 all-gather.3.cloned.1.call-start
  7.2 1.3 convert_element_type.60
  8.5 1.3 collective-permute-start.1
  9.8 5.5 %collective-permute-start = (bf16[1024,256]{1,0:T(8,128)(2,1)S(1)}, bf16[1024,256]{1,0:T(8,128)(2,1)S(1)}, u32[]{:S(2)}, u32[]{:S(2)}) collective-permute-start(bf16[1024,256]{1,0:T(8,128)(2,1)S(1)} %convert_element_type.60), channel_id=1, source_target_pairs={{0,4},{4,8},{8,12},{12,16},{16,20},{20,24},{24,28},{1,5},{5,9},{9,... | collective-permute-start | bytes 1572872 | tf_op jit(solution)/shard_map/ppermute | solution.py:21
  15.3 0.7 compare_select_fusion.1
  16.0 0.7 broadcast_clamp_fusion
  16.7 8.6 %collective-permute-done.1 = bf16[1024,256]{1,0:T(8,128)(2,1)S(1)} collective-permute-done((bf16[1024,256]{1,0:T(8,128)(2,1)S(1)}, bf16[1024,256]{1,0:T(8,128)(2,1)S(1)}, u32[]{:S(2)}, u32[]{:S(2)}) %collective-permute-start.1) | collective-permute-done | bytes 524320 | tf_op jit(solution)/shard_map/ppermute | solution.py:23
  25.3 11.4 %collective-permute-done = bf16[1024,256]{1,0:T(8,128)(2,1)S(1)} collective-permute-done((bf16[1024,256]{1,0:T(8,128)(2,1)S(1)}, bf16[1024,256]{1,0:T(8,128)(2,1)S(1)}, u32[]{:S(2)}, u32[]{:S(2)}) %collective-permute-start) | collective-permute-done | bytes 524320 | tf_op jit(solution)/shard_map/ppermute | solution.py:21
  36.7 0.1 pad_maximum_fusion
  36.8 0.0 copy-start.3
  36.8 7.5 %gather_fusion = bf16[2048,256]{1,0:T(8,128)(2,1)S(1)} fusion(bf16[3072,256]{1,0:T(8,128)(2,1)S(1)} %pad_maximum_fusion, s32[2048]{0:T(1024)S(1)} %get-tuple-element.8), kind=kCustom, calls=%fused_computation | custom fusion | bytes 2105344 | tf_op jit(solution)/shard_map/gather | solution.py:46
  44.3 0.0 copy-done.3
  44.3 0.3 multiply_convert_fusion.1
  44.6 0.6 gather_fusion.1
  45.3 0.0 copy-start.2
  45.3 0.7 copy-done.2
  46.0 0.0 all-gather.3.cloned.1.call-update
  46.0 0.0 all-gather.5.cloned.1.call-start
  46.0 5.8 %fusion.13 = f32[256,2048]{1,0:T(8,128)S(1)} fusion(bf16[2048,256]{1,0:T(8,128)(2,1)S(1)} %multiply_convert_fusion.1, bf16[2048,2048]{1,0:T(8,128)(2,1)} %param.8), kind=kOutput, calls=%fused_computation.35 | convolution fusion | flops 2147483648 | bytes 11534336 | tf_op jit(solution)/shard_map/dot_general | solution.py:56
  51.8 0.0 copy-start.4
  51.8 73.1 %all-gather.3.cloned.1.call-done = bf16[32,512,256]{2,1,0:T(8,128)(2,1)} async-done(((bf16[1,512,256]{2,1,0:T(8,128)(2,1)}), bf16[32,512,256]{2,1,0:T(8,128)(2,1)}) %all-gather.3.cloned.1.call-update) | async-done | bytes 8388624 | tf_op jit(solution)/shard_map/all_gather | solution.py:8
  124.9 4.7 %reduce_sum.24 = bf16[512,256]{1,0:T(8,128)(2,1)S(1)} reduce(bf16[32,512,256]{2,1,0:T(8,128)(2,1)} %all-gather.3.cloned.1.call-done, bf16[]{:T(256)} %constant.10.clone.1), dimensions={0}, to_apply=%region_0.0 | reduce | flops 4063232 | bytes 8650754 | tf_op jit(solution)/shard_map/reduce_sum | solution.py:9
  129.7 0.0 copy-done
  129.7 0.0 copy-done.4
  129.7 0.7 fusion.5
  130.4 0.5 copy.11
  131.0 9.8 %scatter_custom_fusion = bf16[3072,256]{1,0:T(8,128)(2,1)S(1)} fusion(s32[2048]{0:T(1024)S(1)} %get-tuple-element.9, bf16[2048,256]{1,0:T(8,128)(2,1)S(1)} %copy.11, bf16[]{:T(256)} %constant.10.clone.1), kind=kCustom, calls=%fused_computation.24 | custom fusion | bytes 1572866 | tf_op jit(solution)/shard_map/scatter | solution.py:62
  140.8 0.1 fusion.12
  140.8 1.3 collective-permute-start.2
  142.1 4.6 %collective-permute-start.3 = (bf16[1024,256]{1,0:T(8,128)(2,1)S(1)}, bf16[1024,256]{1,0:T(8,128)(2,1)S(1)}, u32[]{:S(2)}, u32[]{:S(2)}) collective-permute-start(bf16[1024,256]{1,0:T(8,128)(2,1)S(1)} %get-tuple-element.7), channel_id=1, source_target_pairs={{0,4},{4,8},{8,12},{12,16},{16,20},{20,24},{24,28},{1,5},{5,9},{9,... | collective-permute-start | bytes 1572872 | tf_op jit(solution)/shard_map/ppermute | solution.py:33
  146.7 10.1 %collective-permute-done.2 = bf16[1024,256]{1,0:T(8,128)(2,1)S(1)} collective-permute-done((bf16[1024,256]{1,0:T(8,128)(2,1)S(1)}, bf16[1024,256]{1,0:T(8,128)(2,1)S(1)}, u32[]{:S(2)}, u32[]{:S(2)}) %collective-permute-start.2) | collective-permute-done | bytes 524320 | tf_op jit(solution)/shard_map/ppermute | solution.py:33
  156.8 11.1 %collective-permute-done.3 = bf16[1024,256]{1,0:T(8,128)(2,1)S(1)} collective-permute-done((bf16[1024,256]{1,0:T(8,128)(2,1)S(1)}, bf16[1024,256]{1,0:T(8,128)(2,1)S(1)}, u32[]{:S(2)}, u32[]{:S(2)}) %collective-permute-start.3) | collective-permute-done | bytes 524320 | tf_op jit(solution)/shard_map/ppermute | solution.py:33
  167.9 1.2 fusion.10
  169.1 1.3 collective-permute-start.5
  170.3 5.2 %collective-permute-start.4 = (bf16[1024,256]{1,0:T(8,128)(2,1)S(1)}, bf16[1024,256]{1,0:T(8,128)(2,1)S(1)}, u32[]{:S(2)}, u32[]{:S(2)}) collective-permute-start(bf16[1024,256]{1,0:T(8,128)(2,1)S(1)} %get-tuple-element.2), channel_id=1, source_target_pairs={{0,4},{4,8},{8,12},{12,16},{16,20},{20,24},{24,28},{1,5},{5,9},{9,... | collective-permute-start | bytes 1572872 | tf_op jit(solution)/shard_map/ppermute | solution.py:21
  175.6 10.0 %collective-permute-done.5 = bf16[1024,256]{1,0:T(8,128)(2,1)S(1)} collective-permute-done((bf16[1024,256]{1,0:T(8,128)(2,1)S(1)}, bf16[1024,256]{1,0:T(8,128)(2,1)S(1)}, u32[]{:S(2)}, u32[]{:S(2)}) %collective-permute-start.5) | collective-permute-done | bytes 524320 | tf_op jit(solution)/shard_map/ppermute | solution.py:23
  185.5 11.4 %collective-permute-done.4 = bf16[1024,256]{1,0:T(8,128)(2,1)S(1)} collective-permute-done((bf16[1024,256]{1,0:T(8,128)(2,1)S(1)}, bf16[1024,256]{1,0:T(8,128)(2,1)S(1)}, u32[]{:S(2)}, u32[]{:S(2)}) %collective-permute-start.4) | collective-permute-done | bytes 524320 | tf_op jit(solution)/shard_map/ppermute | solution.py:21
  196.9 0.1 pad_maximum_fusion.1
  197.0 7.5 %gather_fusion.2 = bf16[2048,256]{1,0:T(8,128)(2,1)S(1)} fusion(bf16[3072,256]{1,0:T(8,128)(2,1)S(1)} %pad_maximum_fusion.1, s32[2048]{0:T(1024)S(1)} %get-tuple-element.8), kind=kCustom, calls=%fused_computation.2 | custom fusion | bytes 2105344 | tf_op jit(solution)/shard_map/gather | solution.py:46
  204.5 0.3 multiply_convert_fusion
  204.9 0.6 gather_fusion.3
  205.5 0.0 copy-start.1
  205.5 0.7 copy-done.1
  206.2 0.0 all-gather.5.cloned.1.call-update
  206.2 5.8 %fusion.14 = f32[256,2048]{1,0:T(8,128)S(1)} fusion(bf16[2048,256]{1,0:T(8,128)(2,1)S(1)} %multiply_convert_fusion, bf16[2048,2048]{1,0:T(8,128)(2,1)} %param.8), kind=kOutput, calls=%fused_computation.36 | convolution fusion | flops 2147483648 | bytes 11534336 | tf_op jit(solution)/shard_map/dot_general | solution.py:56
  212.0 71.6 %all-gather.5.cloned.1.call-done = bf16[32,512,256]{2,1,0:T(8,128)(2,1)} async-done(((bf16[1,512,256]{2,1,0:T(8,128)(2,1)}), bf16[32,512,256]{2,1,0:T(8,128)(2,1)}) %all-gather.5.cloned.1.call-update) | async-done | bytes 8388624 | tf_op jit(solution)/shard_map/all_gather | solution.py:8
  283.6 4.7 %reduce_sum.25 = bf16[512,256]{1,0:T(8,128)(2,1)S(1)} reduce(bf16[32,512,256]{2,1,0:T(8,128)(2,1)} %all-gather.5.cloned.1.call-done, bf16[]{:T(256)} %constant.10.clone.1), dimensions={0}, to_apply=%region_2.0 | reduce | flops 4063232 | bytes 8650754 | tf_op jit(solution)/shard_map/reduce_sum | solution.py:9
  288.3 0.7 fusion.4
  289.1 0.5 copy.12
  289.6 9.8 %scatter_custom_fusion.1 = bf16[3072,256]{1,0:T(8,128)(2,1)S(1)} fusion(s32[2048]{0:T(1024)S(1)} %get-tuple-element.9, bf16[2048,256]{1,0:T(8,128)(2,1)S(1)} %copy.12, bf16[]{:T(256)} %constant.10.clone.1), kind=kCustom, calls=%fused_computation.22 | custom fusion | bytes 1572866 | tf_op jit(solution)/shard_map/scatter | solution.py:62
  299.4 0.1 fusion.11
  299.5 1.3 collective-permute-start.6
  300.8 4.6 %collective-permute-start.7 = (bf16[1024,256]{1,0:T(8,128)(2,1)S(1)}, bf16[1024,256]{1,0:T(8,128)(2,1)S(1)}, u32[]{:S(2)}, u32[]{:S(2)}) collective-permute-start(bf16[1024,256]{1,0:T(8,128)(2,1)S(1)} %get-tuple-element.5), channel_id=1, source_target_pairs={{0,4},{4,8},{8,12},{12,16},{16,20},{20,24},{24,28},{1,5},{5,9},{9,... | collective-permute-start | bytes 1572872 | tf_op jit(solution)/shard_map/ppermute | solution.py:33
  305.4 10.1 %collective-permute-done.6 = bf16[1024,256]{1,0:T(8,128)(2,1)S(1)} collective-permute-done((bf16[1024,256]{1,0:T(8,128)(2,1)S(1)}, bf16[1024,256]{1,0:T(8,128)(2,1)S(1)}, u32[]{:S(2)}, u32[]{:S(2)}) %collective-permute-start.6) | collective-permute-done | bytes 524320 | tf_op jit(solution)/shard_map/ppermute | solution.py:33
  315.5 11.1 %collective-permute-done.7 = bf16[1024,256]{1,0:T(8,128)(2,1)S(1)} collective-permute-done((bf16[1024,256]{1,0:T(8,128)(2,1)S(1)}, bf16[1024,256]{1,0:T(8,128)(2,1)S(1)}, u32[]{:S(2)}, u32[]{:S(2)}) %collective-permute-start.7) | collective-permute-done | bytes 524320 | tf_op jit(solution)/shard_map/ppermute | solution.py:33
  326.5 1.1 convert_add_fusion
  (5 shorter events, 0.1 us)
Async XLA Ops:
  7.2 122.5 %copy-start = (bf16[16,2048]{1,0:T(8,128)(2,1)S(1)}, bf16[16,2048]{1,0:T(8,128)(2,1)}, u32[]{:S(2)}) copy-start(bf16[16,2048]{1,0:T(8,128)(2,1)} %param.9) | copy-start | bytes 196612
  7.2 117.8 %all-gather.3.cloned.1.call-start = ((), (), s32[]{:S(2)}) async-start(), calls=%async_computation | async-start | bytes 8650752 | tf_op jit(solution)/shard_map/all_gather | solution.py:8
  8.5 16.8 %collective-permute-start.1 = (bf16[1024,256]{1,0:T(8,128)(2,1)S(1)}, bf16[1024,256]{1,0:T(8,128)(2,1)S(1)}, u32[]{:S(2)}, u32[]{:S(2)}) collective-permute-start(bf16[1024,256]{1,0:T(8,128)(2,1)S(1)} %convert_element_type.60), channel_id=1, source_target_pairs={{4,0},{8,4},{12,8},{16,12},{20,16},{24,20},{28,24},{5,1},{9,5},{13... | collective-permute-start | bytes 1572872 | tf_op jit(solution)/shard_map/ppermute | solution.py:23
  9.8 26.8 %collective-permute-start = (bf16[1024,256]{1,0:T(8,128)(2,1)S(1)}, bf16[1024,256]{1,0:T(8,128)(2,1)S(1)}, u32[]{:S(2)}, u32[]{:S(2)}) collective-permute-start(bf16[1024,256]{1,0:T(8,128)(2,1)S(1)} %convert_element_type.60), channel_id=1, source_target_pairs={{0,4},{4,8},{8,12},{12,16},{16,20},{20,24},{24,28},{1,5},{5,9},{9,... | collective-permute-start | bytes 1572872 | tf_op jit(solution)/shard_map/ppermute | solution.py:21
  36.8 7.5 %copy-start.3 = (f32[2048]{0:T(1024)S(1)}, f32[2048]{0:T(1024)}, u32[]{:S(2)}) copy-start(f32[2048]{0:T(1024)} %param.10) | copy-start | bytes 24580
  45.3 0.7 copy-start.2
  46.0 237.6 %all-gather.5.cloned.1.call-start = ((), (), s32[]{:S(2)}) async-start(), calls=%async_computation.1 | async-start | bytes 8650752 | tf_op jit(solution)/shard_map/all_gather | solution.py:8
  51.8 77.9 %copy-start.4 = (bf16[16,512]{1,0:T(8,128)(2,1)S(1)}, bf16[16,512]{1,0:T(8,128)(2,1)}, u32[]{:S(2)}) copy-start(bf16[16,512]{1,0:T(8,128)(2,1)} %param.11) | copy-start | bytes 49156
  140.8 16.0 %collective-permute-start.2 = (bf16[1024,256]{1,0:T(8,128)(2,1)S(1)}, bf16[1024,256]{1,0:T(8,128)(2,1)S(1)}, u32[]{:S(2)}, u32[]{:S(2)}) collective-permute-start(bf16[1024,256]{1,0:T(8,128)(2,1)S(1)} %get-tuple-element.6), channel_id=1, source_target_pairs={{4,0},{8,4},{12,8},{16,12},{20,16},{24,20},{28,24},{5,1},{9,5},{13... | collective-permute-start | bytes 1572872 | tf_op jit(solution)/shard_map/ppermute | solution.py:33
  142.1 25.8 %collective-permute-start.3 = (bf16[1024,256]{1,0:T(8,128)(2,1)S(1)}, bf16[1024,256]{1,0:T(8,128)(2,1)S(1)}, u32[]{:S(2)}, u32[]{:S(2)}) collective-permute-start(bf16[1024,256]{1,0:T(8,128)(2,1)S(1)} %get-tuple-element.7), channel_id=1, source_target_pairs={{0,4},{4,8},{8,12},{12,16},{16,20},{20,24},{24,28},{1,5},{5,9},{9,... | collective-permute-start | bytes 1572872 | tf_op jit(solution)/shard_map/ppermute | solution.py:33
  169.1 16.5 %collective-permute-start.5 = (bf16[1024,256]{1,0:T(8,128)(2,1)S(1)}, bf16[1024,256]{1,0:T(8,128)(2,1)S(1)}, u32[]{:S(2)}, u32[]{:S(2)}) collective-permute-start(bf16[1024,256]{1,0:T(8,128)(2,1)S(1)} %get-tuple-element.2), channel_id=1, source_target_pairs={{4,0},{8,4},{12,8},{16,12},{20,16},{24,20},{28,24},{5,1},{9,5},{13... | collective-permute-start | bytes 1572872 | tf_op jit(solution)/shard_map/ppermute | solution.py:23
  170.3 26.6 %collective-permute-start.4 = (bf16[1024,256]{1,0:T(8,128)(2,1)S(1)}, bf16[1024,256]{1,0:T(8,128)(2,1)S(1)}, u32[]{:S(2)}, u32[]{:S(2)}) collective-permute-start(bf16[1024,256]{1,0:T(8,128)(2,1)S(1)} %get-tuple-element.2), channel_id=1, source_target_pairs={{0,4},{4,8},{8,12},{12,16},{16,20},{20,24},{24,28},{1,5},{5,9},{9,... | collective-permute-start | bytes 1572872 | tf_op jit(solution)/shard_map/ppermute | solution.py:21
  205.5 0.7 copy-start.1
  299.5 16.0 %collective-permute-start.6 = (bf16[1024,256]{1,0:T(8,128)(2,1)S(1)}, bf16[1024,256]{1,0:T(8,128)(2,1)S(1)}, u32[]{:S(2)}, u32[]{:S(2)}) collective-permute-start(bf16[1024,256]{1,0:T(8,128)(2,1)S(1)} %get-tuple-element.4), channel_id=1, source_target_pairs={{4,0},{8,4},{12,8},{16,12},{20,16},{24,20},{28,24},{5,1},{9,5},{13... | collective-permute-start | bytes 1572872 | tf_op jit(solution)/shard_map/ppermute | solution.py:33
  300.8 25.8 %collective-permute-start.7 = (bf16[1024,256]{1,0:T(8,128)(2,1)S(1)}, bf16[1024,256]{1,0:T(8,128)(2,1)S(1)}, u32[]{:S(2)}, u32[]{:S(2)}) collective-permute-start(bf16[1024,256]{1,0:T(8,128)(2,1)S(1)} %get-tuple-element.5), channel_id=1, source_target_pairs={{0,4},{4,8},{8,12},{12,16},{16,20},{20,24},{24,28},{1,5},{5,9},{9,... | collective-permute-start | bytes 1572872 | tf_op jit(solution)/shard_map/ppermute | solution.py:33
Sparse Core Ops, SparseCore 0:
  46.1 78.7 all-gather.2
  206.4 77.1 all-gather.4
